TPU v7x, 512 devices: a whole 4x4x16 slice. The times are simulated.
512 devices in a mesh: dp: 4 (over z_hi, core), tm: 8 (over z_lo), height: 16 (over x, y).
Axes of the slice: x: 4, y: 4, z: 16 (z_hi: 2, z_lo: 8; z = z_hi * 8 + z_lo), core: 2. Of those that a mesh axis runs over, the one named last changes fastest.
Arguments:
- clips: bfloat16 [4, 16, 64, 128, 128], P('dp', 'tm', 'height'), may hold values from -6 to 6
- frame_counts: int32 [4, 5], P('dp'), may hold values from 1 to 9, 16 in all within a row
- conv_first: bfloat16 [3, 3, 3, 128, 128], replicated, may hold values from -0.109375 to 0.109375
- conv_down: bfloat16 [3, 3, 3, 128, 128], replicated, may hold values from -0.109375 to 0.109375
- out_cotangent: bfloat16 [4, 8, 32, 64, 128], P('dp', 'tm', 'height'), may hold values from -6 to 6
Outputs:
- encoded: bfloat16 [4, 8, 32, 64, 128], P('dp', 'tm', 'height')
- grad_first: bfloat16 [3, 3, 3, 128, 128], P(None, None, None, 'dp')
- grad_down: bfloat16 [3, 3, 3, 128, 128], P(None, None, None, 'dp')
Inputs may be any that keep to these rules, and one draw needn't show every extreme that they name: `frame_counts`: each sequence's 5 clip lengths sum to 16; in every sequence one clip has exactly 9 frames.
All inputs are finite; a program needn't handle non-finite values.
Results may differ from a plain program's by a relative error of at most 0.0059.
Values may be sent and summed in bfloat16 or wider, within the bound.
No kernel may reach another device: no remote copies, remote signals or barrier semaphores. Data moves between devices by JAX's collectives and lax.ppermute only.
A program may use at most 64 MiB of HBM per device.

v0:
```python
import math
import jax
import jax.numpy as jnp
from jax import lax
from jax.sharding import PartitionSpec as P


def padded_2(cells, sides, width):
    for axis, dim in sides:
        count = lax.axis_size(axis)
        ends = count - 1
        head = lax.slice_in_dim(cells, 0, width, axis=dim)
        tail = lax.slice_in_dim(cells, cells.shape[dim] - width, cells.shape[dim], axis=dim)
        cells = jnp.concatenate(
            [
                lax.ppermute(tail, axis, [(i, (i + 1) % count) for i in range(ends)]),
                cells,
                lax.ppermute(head, axis, [((i + 1) % count, i) for i in range(ends)]),
            ],
            axis=dim,
        )
    return cells


def shifted(value, axis, steps):
    count = lax.axis_size(axis)
    leading, last = (max(0, -steps), min(count, count - steps))
    return lax.ppermute(value, axis, [(source, source + steps) for source in range(leading, last)])


def unfold(frame_slab, stride, pad_cols):
    padded = jnp.pad(frame_slab, ((0, 0), (0, 0), pad_cols, (0, 0)))
    out_rows = (padded.shape[1] - 3) // stride + 1
    out_cols = (padded.shape[2] - 3) // stride + 1
    pieces = []
    for tap_row in range(3):
        for tap_col in range(3):
            pieces.append(
                padded[
                    :,
                    tap_row : tap_row + stride * (out_rows - 1) + 1 : stride,
                    tap_col : tap_col + stride * (out_cols - 1) + 1 : stride,
                ]
            )
    joined = jnp.concatenate(pieces, axis=-1)
    return (joined.reshape(-1, joined.shape[-1]), (frame_slab.shape[0], out_rows, out_cols))


def conv_layer(extended, weight, tap_mask, out_frames, stride, pad_cols):
    channels_out = weight.shape[-1]
    summed = None
    for tap_time in range(3):
        frame_slab = extended[tap_time : tap_time + stride * (out_frames - 1) + 1 : stride]
        columns, shape_out = unfold(frame_slab, stride, pad_cols)
        kernel = weight[tap_time].reshape(-1, channels_out)
        tap_term = jnp.dot(columns, kernel, preferred_element_type=jnp.float32).reshape(
            shape_out + (channels_out,)
        )
        tap_term = tap_term * tap_mask[:, tap_time][:, None, None, None]
        summed = tap_term if summed is None else summed + tap_term
    return summed


def weight_grad(extended, grads, tap_mask, stride, pad_cols):
    out_frames = grads.shape[0]
    blocks = []
    for tap_time in range(3):
        frame_slab = extended[tap_time : tap_time + stride * (out_frames - 1) + 1 : stride]
        columns, shape_out = unfold(frame_slab, stride, pad_cols)
        masked = grads * tap_mask[:, tap_time].astype(jnp.bfloat16)[:, None, None, None]
        blocks.append(
            jnp.dot(
                columns.T, masked.reshape(-1, grads.shape[-1]), preferred_element_type=jnp.float32
            )
        )
    stacked = jnp.stack(blocks)
    return stacked.reshape(3, 3, 3, extended.shape[-1], grads.shape[-1])


def hidden_grad(grads_ext, weight, mask_ext):
    pieces = []
    for tap_time in range(3):
        masked = grads_ext * mask_ext[:, tap_time].astype(jnp.bfloat16)[:, None, None, None]
        kernel = jnp.transpose(weight[tap_time][::-1, ::-1], (0, 1, 3, 2))
        spread = lax.conv_general_dilated(
            masked,
            kernel,
            (1, 1),
            ((2, 0), (2, 2)),
            lhs_dilation=(2, 2),
            dimension_numbers=("NHWC", "HWIO", "NHWC"),
            preferred_element_type=jnp.float32,
        )
        pieces.append(spread[:, 1:, 1:])
    even_frames = pieces[2][:-1] + pieces[0][1:]
    odd_frames = pieces[1][1:]
    merged = jnp.stack([even_frames, odd_frames], axis=1)
    return merged.reshape((2 * even_frames.shape[0],) + even_frames.shape[1:])


def positions(counts_row, frame_index):
    starts = jnp.cumsum(counts_row) - counts_row
    latest = jnp.max(jnp.where(starts[None, :] <= frame_index[:, None], starts[None, :], 0), axis=1)
    return frame_index - latest


def tap_masks(place):
    return (place[:, None] >= (2 - jnp.arange(3, dtype=jnp.int32))[None, :]).astype(jnp.float32)


def body(clips, frame_counts, conv_first, conv_down, out_cotangent):
    frames_dev = clips.shape[1]
    rows_dev = clips.shape[2]
    columns_all = clips.shape[3]
    down_frames = frames_dev // 2
    counts_row = frame_counts[0]
    first_frame = lax.axis_index("tm") * frames_dev
    frame_index = first_frame + jnp.arange(frames_dev, dtype=jnp.int32)
    first_mask = tap_masks(positions(counts_row, frame_index))
    down_index = first_frame + 2 * jnp.arange(down_frames + 1, dtype=jnp.int32)
    mask_ext = tap_masks(positions(counts_row, down_index))
    down_mask = mask_ext[:down_frames]
    with_rows = padded_2(clips[0], (("height", 1),), 1)
    earlier = shifted(with_rows, "tm", 1)
    input_ext = jnp.concatenate([earlier, with_rows], axis=0)
    pre_act = conv_layer(input_ext, conv_first, first_mask, frames_dev, 1, (1, 1))
    hidden = jax.nn.silu(pre_act).astype(jnp.bfloat16)
    above = shifted(hidden[:, rows_dev - 1 :], "height", 1)
    hidden_rows = jnp.concatenate([above, hidden], axis=1)
    hidden_past = shifted(hidden_rows, "tm", 1)
    hidden_ext = jnp.concatenate([hidden_past, hidden_rows], axis=0)
    encoded = conv_layer(hidden_ext, conv_down, down_mask, down_frames, 2, (1, 0)).astype(
        jnp.bfloat16
    )
    cells_all = (
        lax.axis_size("dp")
        * clips.shape[0]
        * down_frames
        * lax.axis_size("tm")
        * (rows_dev // 2)
        * lax.axis_size("height")
        * (columns_all // 2)
    )
    scale = 1.0 / math.sqrt(cells_all)
    grads = (out_cotangent[0].astype(jnp.float32) * scale).astype(jnp.bfloat16)
    down_local = weight_grad(hidden_ext, grads, down_mask, 2, (1, 0))
    below = shifted(grads[:, 0:1], "height", -1)
    grads_rows = jnp.concatenate([grads, below], axis=1)
    grads_next = shifted(grads_rows, "tm", -1)
    grads_ext = jnp.concatenate([grads_rows, grads_next], axis=0)
    back_hidden = hidden_grad(grads_ext, conv_down, mask_ext).astype(jnp.bfloat16)
    sigma = jax.nn.sigmoid(pre_act)
    pre_grad = (back_hidden.astype(jnp.float32) * sigma * (1.0 + pre_act * (1.0 - sigma))).astype(
        jnp.bfloat16
    )
    first_local = weight_grad(input_ext, pre_grad, first_mask, 1, (1, 1))
    share = conv_first.shape[3] // lax.axis_size("dp")
    summed_first, summed_down = lax.psum((first_local, down_local), ("dp", "tm", "height"))
    offset = lax.axis_index("dp") * share
    summed_first = lax.dynamic_slice_in_dim(summed_first, offset, share, 3)
    summed_down = lax.dynamic_slice_in_dim(summed_down, offset, share, 3)
    return (encoded[None], summed_first.astype(jnp.bfloat16), summed_down.astype(jnp.bfloat16))


def solution(mesh):
    in_specs = (
        P("dp", "tm", "height", None, None),
        P("dp", None),
        P(),
        P(),
        P("dp", "tm", "height", None, None),
    )
    out_specs = (
        P("dp", "tm", "height", None, None),
        P(None, None, None, "dp", None),
        P(None, None, None, "dp", None),
    )
    return jax.shard_map(body, mesh=mesh, in_specs=in_specs, out_specs=out_specs, check_vma=False)
```

profile of v0, /device:TPU:32, one launch (start us, length us, event | category | flops | bytes accessed | tf_op | source)
XLA Modules:
  0.0 263.5 jit_solution(3750914941561490961)
XLA Ops:
  0.6 1.0 fusion.93
  1.6 3.5 %collective-permute-start = (bf16[2,1,128,128]{3,2,1,0:T(8,128)(2,1)S(1)}, bf16[2,1,128,128]{3,2,1,0:T(8,128)(2,1)S(1)}, u32[]{:S(2)}, u32[]{:S(2)}) collective-permute-start(bf16[2,1,128,128]{3,2,1,0:T(8,128)(2,1)S(1)} %get-tuple-element.17), channel_id=1, source_target_pairs={{0,1},{1,2},{2,3},{3,4},{4,5},{5,6},{6,7},{7,8},{8,9},{9,10},{10,1... | collective-permute-start | bytes 196616 | tf_op jit(solution)/shard_map/ppermute | solution.py:16
  5.1 1.3 collective-permute-start.1
  6.4 0.8 fusion.63
  7.2 1.3 collective-permute-start.5
  8.5 0.8 reduce-window_clone.1
  9.4 0.7 subtract_bitcast_fusion
  10.4 1.2 fusion.91
  11.6 0.9 fusion.90
  13.1 0.6 slice.447
  13.7 0.6 slice.451
  16.0 5.2 %collective-permute-start.6 = (bf16[1,3,64,128]{3,2,1,0:T(8,128)(2,1)S(1)}, bf16[1,3,64,128]{3,2,1,0:T(8,128)(2,1)S(1)}, u32[]{:S(2)}, u32[]{:S(2)}) collective-permute-start(bf16[1,3,64,128]{3,2,1,0:T(8,128)(2,1)S(1)} %pad_maximum_fusion.7), channel_id=1, source_target_pairs={{16,0},{32,16},{48,32},{64,48},{80,64},{96,80},{112,96},{17,1},{33... | collective-permute-start | bytes 147464 | tf_op jit(solution)/shard_map/ppermute | solution.py:28
  21.3 1.9 collective-permute-start.2
  23.4 1.3 multiply_bitcast_fusion.1
  27.2 3.8 %collective-permute-done.2 = bf16[2,6,128,128]{3,2,1,0:T(8,128)(2,1)S(1)} collective-permute-done((bf16[2,6,128,128]{3,2,1,0:T(8,128)(2,1)S(1)}, bf16[2,6,128,128]{3,2,1,0:T(8,128)(2,1)S(1)}, u32[]{:S(2)}, u32[]{:S(2)}) %collective-permute-start.2) | collective-permute-done | bytes 393248 | tf_op jit(solution)/shard_map/ppermute | solution.py:28
  32.0 0.8 convolution_multiply_fusion.1
  33.7 0.8 fusion.1
  34.5 0.9 fusion.10
  35.5 5.2 %collective-permute-start.3 = (bf16[2,1,128,128]{3,2,1,0:T(8,128)(2,1)S(1)}, bf16[2,1,128,128]{3,2,1,0:T(8,128)(2,1)S(1)}, u32[]{:S(2)}, u32[]{:S(2)}) collective-permute-start(bf16[2,1,128,128]{3,2,1,0:T(8,128)(2,1)S(1)} %slice.437), channel_id=1, source_target_pairs={{0,1},{1,2},{2,3},{3,4},{4,5},{5,6},{6,7},{7,8},{8,9},{9,10},{10,1... | collective-permute-start | bytes 196616 | tf_op jit(solution)/shard_map/ppermute | solution.py:28
  40.7 0.9 fusion.26
  41.5 0.9 fusion.24
  42.4 0.9 fusion.22
  44.8 3.2 %collective-permute-start.4 = (bf16[2,5,128,128]{3,2,1,0:T(8,128)(2,1)S(1)}, bf16[2,5,128,128]{3,2,1,0:T(8,128)(2,1)S(1)}, u32[]{:S(2)}, u32[]{:S(2)}) collective-permute-start(bf16[2,5,128,128]{3,2,1,0:T(8,128)(2,1)S(1)} %pad_maximum_fusion.2), channel_id=1, source_target_pairs={{0,16},{16,32},{32,48},{48,64},{64,80},{80,96},{96,112},{1,17},{17... | collective-permute-start | bytes 983048 | tf_op jit(solution)/shard_map/ppermute | solution.py:28
  48.3 1.1 convolution_bitcast_fusion
  49.4 4.4 %collective-permute-done.4 = bf16[2,5,128,128]{3,2,1,0:T(8,128)(2,1)S(1)} collective-permute-done((bf16[2,5,128,128]{3,2,1,0:T(8,128)(2,1)S(1)}, bf16[2,5,128,128]{3,2,1,0:T(8,128)(2,1)S(1)}, u32[]{:S(2)}, u32[]{:S(2)}) %collective-permute-start.4) | collective-permute-done | bytes 327712 | tf_op jit(solution)/shard_map/ppermute | solution.py:28
  57.8 1.2 pad_maximum_fusion.1
  58.9 196.0 %all-reduce.8 = (bf16[3,3,3,128,128]{4,3,2,1,0:T(8,128)(2,1)}, bf16[3,3,3,128,128]{4,3,2,1,0:T(8,128)(2,1)}) all-reduce(f32[3,3,3,128,128]{4,3,2,1,0:T(8,128)S(1)} %pad_maximum_fusion, f32[3,3,3,128,128]{4,3,2,1,0:T(8,128)S(1)} %pad_maximum_fusion.1), channel_id=1, replica_groups=mesh['dp'=4,'tm'=8,'height'=16] {'dp','tm','height'}, use_global_device_ids=true, to_apply=%region_3.4 | all-reduce | flops 884736 | bytes 5308416 | tf_op jit(solution)/shard_map/psum | solution.py:158
  255.0 1.7 dynamic-slice_convert_fusion
  256.7 1.6 dynamic-slice_convert_fusion.1
  258.3 1.8 convolution_multiply_fusion.5
  260.1 1.9 fusion.6
  262.1 1.4 fusion.8
  (154 shorter events, 10.4 us)
Async XLA Ops:
  0.6 20.6 %copy-start = (bf16[1,2,4,128,128]{4,3,2,1,0:T(8,128)(2,1)S(1)}, bf16[1,2,4,128,128]{4,3,2,1,0:T(8,128)(2,1)}, u32[]{:S(2)}) copy-start(bf16[1,2,4,128,128]{4,3,2,1,0:T(8,128)(2,1)} %param.5) | copy-start | bytes 786436
  0.6 10.9 %copy-start.6 = (bf16[3,3,3,128,128]{4,3,2,1,0:T(8,128)(2,1)S(1)}, bf16[3,3,3,128,128]{4,3,2,1,0:T(8,128)(2,1)}, u32[]{:S(2)}) copy-start(bf16[3,3,3,128,128]{4,3,2,1,0:T(8,128)(2,1)} %param.8) | copy-start | bytes 2654212
  1.6 19.6 %collective-permute-start = (bf16[2,1,128,128]{3,2,1,0:T(8,128)(2,1)S(1)}, bf16[2,1,128,128]{3,2,1,0:T(8,128)(2,1)S(1)}, u32[]{:S(2)}, u32[]{:S(2)}) collective-permute-start(bf16[2,1,128,128]{3,2,1,0:T(8,128)(2,1)S(1)} %get-tuple-element.17), channel_id=1, source_target_pairs={{0,1},{1,2},{2,3},{3,4},{4,5},{5,6},{6,7},{7,8},{8,9},{9,10},{10,1... | collective-permute-start | bytes 196616 | tf_op jit(solution)/shard_map/ppermute | solution.py:16
  5.1 16.1 %collective-permute-start.1 = (bf16[2,1,128,128]{3,2,1,0:T(8,128)(2,1)S(1)}, bf16[2,1,128,128]{3,2,1,0:T(8,128)(2,1)S(1)}, u32[]{:S(2)}, u32[]{:S(2)}) collective-permute-start(bf16[2,1,128,128]{3,2,1,0:T(8,128)(2,1)S(1)} %get-tuple-element.18), channel_id=1, source_target_pairs={{1,0},{2,1},{3,2},{4,3},{5,4},{6,5},{7,6},{8,7},{9,8},{10,9},{11,1... | collective-permute-start | bytes 196616 | tf_op jit(solution)/shard_map/ppermute | solution.py:18
  7.2 8.8 %collective-permute-start.5 = (bf16[1,1,64,128]{3,2,1,0:T(8,128)(2,1)S(1)}, bf16[1,1,64,128]{3,2,1,0:T(8,128)(2,1)S(1)}, u32[]{:S(2)}, u32[]{:S(2)}) collective-permute-start(bf16[1,1,64,128]{3,2,1,0:T(8,128)(2,1)S(1)} %slice.442), channel_id=1, source_target_pairs={{1,0},{2,1},{3,2},{4,3},{5,4},{6,5},{7,6},{8,7},{9,8},{10,9},{11,1... | collective-permute-start | bytes 49160 | tf_op jit(solution)/shard_map/ppermute | solution.py:28
  11.6 13.5 %copy-start.8 = (pred[8,18]{0,1:T(8,128)(4,1)S(1)}, pred[8,18]{0,1:T(8,128)(4,1)}, u32[]{:S(2)}) copy-start(pred[8,18]{0,1:T(8,128)(4,1)} %constant.62) | copy-start | bytes 436
  16.0 7.3 %collective-permute-start.6 = (bf16[1,3,64,128]{3,2,1,0:T(8,128)(2,1)S(1)}, bf16[1,3,64,128]{3,2,1,0:T(8,128)(2,1)S(1)}, u32[]{:S(2)}, u32[]{:S(2)}) collective-permute-start(bf16[1,3,64,128]{3,2,1,0:T(8,128)(2,1)S(1)} %pad_maximum_fusion.7), channel_id=1, source_target_pairs={{16,0},{32,16},{48,32},{64,48},{80,64},{96,80},{112,96},{17,1},{33... | collective-permute-start | bytes 147464 | tf_op jit(solution)/shard_map/ppermute | solution.py:28
  21.3 9.7 %collective-permute-start.2 = (bf16[2,6,128,128]{3,2,1,0:T(8,128)(2,1)S(1)}, bf16[2,6,128,128]{3,2,1,0:T(8,128)(2,1)S(1)}, u32[]{:S(2)}, u32[]{:S(2)}) collective-permute-start(bf16[2,6,128,128]{3,2,1,0:T(8,128)(2,1)S(1)} %pad_maximum_fusion.3), channel_id=1, source_target_pairs={{0,16},{16,32},{32,48},{48,64},{64,80},{80,96},{96,112},{1,17},{17... | collective-permute-start | bytes 1179656 | tf_op jit(solution)/shard_map/ppermute | solution.py:28
  35.5 8.0 %collective-permute-start.3 = (bf16[2,1,128,128]{3,2,1,0:T(8,128)(2,1)S(1)}, bf16[2,1,128,128]{3,2,1,0:T(8,128)(2,1)S(1)}, u32[]{:S(2)}, u32[]{:S(2)}) collective-permute-start(bf16[2,1,128,128]{3,2,1,0:T(8,128)(2,1)S(1)} %slice.437), channel_id=1, source_target_pairs={{0,1},{1,2},{2,3},{3,4},{4,5},{5,6},{6,7},{7,8},{8,9},{9,10},{10,1... | collective-permute-start | bytes 196616 | tf_op jit(solution)/shard_map/ppermute | solution.py:28
  43.5 4.9 %copy-start.7 = (bf16[1,1,2,64,128]{4,3,2,1,0:T(8,128)(2,1)S(1)}, bf16[1,1,2,64,128]{4,3,2,1,0:T(8,128)(2,1)}, u32[]{:S(2)}) copy-start(bf16[1,1,2,64,128]{4,3,2,1,0:T(8,128)(2,1)} %param.9) | copy-start | bytes 98308
  44.8 9.0 %collective-permute-start.4 = (bf16[2,5,128,128]{3,2,1,0:T(8,128)(2,1)S(1)}, bf16[2,5,128,128]{3,2,1,0:T(8,128)(2,1)S(1)}, u32[]{:S(2)}, u32[]{:S(2)}) collective-permute-start(bf16[2,5,128,128]{3,2,1,0:T(8,128)(2,1)S(1)} %pad_maximum_fusion.2), channel_id=1, source_target_pairs={{0,16},{16,32},{32,48},{48,64},{64,80},{80,96},{96,112},{1,17},{17... | collective-permute-start | bytes 983048 | tf_op jit(solution)/shard_map/ppermute | solution.py:28
  48.2 8.4 %copy-start.1 = (bf16[1,2,64,1152]{3,2,1,0:T(8,128)(2,1)}, bf16[1,2,64,1152]{3,2,1,0:T(8,128)(2,1)S(1)}, u32[]{:S(2)}) copy-start(bf16[1,2,64,1152]{3,2,1,0:T(8,128)(2,1)S(1)} %constant_dynamic-update-slice_fusion.19) | copy-start | bytes 884740
  56.5 0.7 copy-start.3
  56.8 0.7 copy-start.4
  255.0 7.1 %copy-start.2 = (bf16[1,2,64,1152]{3,2,1,0:T(8,128)(2,1)S(1)}, bf16[1,2,64,1152]{3,2,1,0:T(8,128)(2,1)}, u32[]{:S(2)}) copy-start(bf16[1,2,64,1152]{3,2,1,0:T(8,128)(2,1)} %copy-done.1) | copy-start | bytes 884740
  255.0 7.1 %copy-start.5 = (bf16[1,3,3,128,128]{4,3,2,1,0:T(8,128)(2,1)S(1)}, bf16[1,3,3,128,128]{4,3,2,1,0:T(8,128)(2,1)}, u32[]{:S(2)}) copy-start(bf16[1,3,3,128,128]{4,3,2,1,0:T(8,128)(2,1)} %get-tuple-element.7) | copy-start | bytes 884740
where the time goes:
time: 264 us; the launch traced here: 263 us
  blocking collectives  196 us (74%)
  starting transfers between devices  21.6 us (8%)
  local copies, waits for them, and re-layouts  15.7 us (6%)
  matrix products  12.9 us (5%)
  waiting for transfers between devices  8.16 us (3%)
  other arithmetic  5.58 us (2%)
  between operations  3.58 us (1%)
    psum x1, blocking collectives, body(): lax.psum((first_local, down_local), ('dp', 'tm', 'height'))  196 us
    ppermute x5, starting transfers between devices, shifted(): lax.ppermute(value, axis, [(source, source + steps) for source in range(l...  16.8 us
    ppermute x5, waiting for transfers between devices, shifted(): lax.ppermute(value, axis, [(source, source + steps) for source in range(l...  8.16 us
    dot_general x6, matrix products, conv_layer(): jnp.dot(columns, kernel, preferred_element_type=jnp.float32)  7.65 us
  transfers between devices with their start and end apart: 7, of which 2 were waited for; matrix products, arithmetic and copies ran while one was open for 5% of the time, Pallas kernels for 0%

commit v1 on v0

--- a/solution.py
+++ b/solution.py
@@ -155,7 +155,9 @@
     )
     first_local = weight_grad(input_ext, pre_grad, first_mask, 1, (1, 1))
     share = conv_first.shape[3] // lax.axis_size("dp")
-    summed_first, summed_down = lax.psum((first_local, down_local), ("dp", "tm", "height"))
+    summed_first, summed_down = lax.psum(
+        lax.psum((first_local, down_local), "dp"), ("tm", "height")
+    )
     offset = lax.axis_index("dp") * share
     summed_first = lax.dynamic_slice_in_dim(summed_first, offset, share, 3)
     summed_down = lax.dynamic_slice_in_dim(summed_down, offset, share, 3)

time: 264 us -> 1420 us (5.38)
  the two profiles are of different devices: /device:TPU:32 before, /device:TPU:0 now
where the time goes in v1:
time: 1420 us
  blocking collectives  1080 us (76%)
  waiting for transfers between devices  276 us (19%)
  starting transfers between devices  19.5 us (1%)
  between operations  17.1 us (1%)
    psum x1, blocking collectives, body(): lax.psum(lax.psum((first_local, down_local), 'dp'), ('tm', 'height'))  1080 us
    psum x1, waiting for transfers between devices, body(): lax.psum((first_local, down_local), 'dp')  271 us
  transfers between devices with their start and end apart: 8, of which 3 were waited for; matrix products, arithmetic and copies ran while one was open for 1% of the time, Pallas kernels for 0%

profile of v1, /device:TPU:0, one launch (start us, length us, event | category | flops | bytes accessed | tf_op | source)
XLA Modules:
  0.0 1418.4 jit_solution(15799844720236836351)
XLA Ops:
  7.2 0.9 fusion.93
  8.1 1.3 collective-permute-start
  9.4 1.3 collective-permute-start.1
  10.7 0.8 fusion.63
  11.5 1.3 collective-permute-start.5
  12.9 0.8 reduce-window_clone.1
  13.7 0.7 subtract_bitcast_fusion
  14.7 1.3 fusion.91
  16.0 0.6 fusion.94
  16.6 0.6 slice.447
  19.7 1.3 collective-permute-start.6
  21.1 4.6 collective-permute-start.2
  25.8 1.3 multiply_bitcast_fusion.1
  29.6 1.3 collective-permute-done.2
  32.0 0.8 convolution_multiply_fusion.1
  33.7 0.8 fusion.1
  34.4 0.9 fusion.10
  35.4 5.2 collective-permute-start.3
  40.6 0.9 fusion.26
  41.5 0.9 fusion.24
  42.3 0.9 fusion.22
  43.2 1.4 pad_maximum_fusion
  45.9 4.6 collective-permute-start.4
  51.0 3.9 collective-permute-done.4
  58.5 1.4 pad_maximum_fusion.1
  60.0 0.8 convolution_multiply_fusion.5
  60.8 0.9 fusion.6
  61.7 1.5 fusion.8
  63.2 271.1 %all-reduce.11.cloned.1.call-done = (f32[3,3,3,128,128]{4,3,2,1,0:T(8,128)}, f32[3,3,3,128,128]{4,3,2,1,0:T(8,128)}) async-done(((f32[3,3,3,128,128]{4,3,2,1,0:T(8,128)}, f32[3,3,3,128,128]{4,3,2,1,0:T(8,128)}), (f32[3,3,3,128,128]{4,3,2,1,0:T(8,128)}, f32[3,3,3,128,128]{4,3,2,1,0:T(8,128)})) %all-reduce.11.cloned.1.call-update) | async-done | bytes 3538960 | tf_op jit(solution)/shard_map/psum | solution.py:159
  334.3 1075.8 %all-reduce.12 = (bf16[3,3,3,128,128]{4,3,2,1,0:T(8,128)(2,1)S(1)}, bf16[3,3,3,128,128]{4,3,2,1,0:T(8,128)(2,1)S(1)}) all-reduce(f32[3,3,3,128,128]{4,3,2,1,0:T(8,128)} %get-tuple-element.7, f32[3,3,3,128,128]{4,3,2,1,0:T(8,128)} %get-tuple-element.8), channel_id=1, replica_groups=mesh['dp'=4,'tm'=8,'height'=16] {'tm','height'}, use_global_device_ids=true, to_apply=%region_4.5 | all-reduce | flops 884736 | bytes 5308416 | tf_op jit(solution)/shard_map/psum | solution.py:158
  1410.1 0.7 dynamic-slice_convert_fusion
  1410.8 0.7 dynamic-slice_convert_fusion.1
  (147 shorter events, 10.3 us)
Async XLA Ops:
  7.2 13.9 copy-start
  7.2 327.2 %all-reduce.11.cloned.1.call-start = ((), (), s32[]{:S(2)}) async-start(), calls=%async_computation | async-start | bytes 7077888 | tf_op jit(solution)/shard_map/psum | solution.py:159
  8.1 12.9 collective-permute-start
  9.4 11.6 collective-permute-start.1
  11.5 8.2 collective-permute-start.5
  14.7 12.8 copy-start.1
  14.7 12.8 copy-start.3
  19.7 6.1 collective-permute-start.6
  21.1 9.8 collective-permute-start.2
  35.4 9.2 collective-permute-start.3
  44.6 6.2 copy-start.2
  45.9 9.0 collective-permute-start.4
Sparse Core Ops, SparseCore 0:
  60.0 274.2 all-reduce.10
